TPU v7x, 32 devices: a whole 2x2x4 slice. The times are simulated.
32 devices in a mesh: sta: 8 (over z, x), tm: 4 (over y, core).
Axes of the slice: x: 2, y: 2, z: 4, core: 2. Of those that a mesh axis runs over, the one named last changes fastest.
Arguments:
- records: float32 [16, 1, 65536], P('sta', None, 'tm'), may hold values from -6 to 6
- pair_blocks: int32 [24, 2], P('sta'), may hold values from 0 to 7, as said below
- pair_count: int32 [8], P('sta'), may hold values from 0 to 3, as said below
Outputs:
- correlations: float32 [24, 2, 2, 2048], P('sta', None, None, 'tm')
Inputs may be any that keep to these rules, and one draw needn't show every extreme that they name: `pair_blocks`: slot q belongs to owner o = q // 3. Every slot names blocks a <= b with o <= a and b <= o + 3, both below 8; the slots in use have a < b. `pair_count`: an owner with no higher block within 3 has no slot in use.
All inputs are finite; a program needn't handle non-finite values.
Results may differ from a plain program's by a relative error of at most 0.0003.
Values sent between devices are 32-bit elements; how exact they have to be, the bound alone decides.
No kernel may reach another device: no remote copies, remote signals or barrier semaphores. Data moves between devices by JAX's collectives and lax.ppermute only.
A program may use at most 64 MiB of HBM per device.

v0:
```python
import math
import jax
import jax.numpy as jnp
from jax import lax
from jax.sharding import PartitionSpec as P

SAMPLES = 65536
FACTOR_A = 256
BAND = 32
LAGS = 4
REACH = 3
highest = lax.Precision.HIGHEST
epsilon = 1e-06


def passed_along(block, axis, distance):
    devices = range(lax.axis_size(axis))
    route = [(i - distance, i) for i in devices if i - distance in devices]
    return lax.ppermute(block, axis, route)


def angles(row_ids, col_ids, modulus):
    product = row_ids[:, None] * col_ids[None, :] % modulus
    radians = product.astype(jnp.float32) * (2.0 * math.pi / modulus)
    return (jnp.cos(radians), jnp.sin(radians))


def matmul(left_mat, right_mat):
    return jnp.dot(left_mat, right_mat, precision=highest, preferred_element_type=jnp.float32)


def local(records, pair_blocks, pair_count):
    stations, hour_count, time_cols = records.shape
    time_devices = lax.axis_size("tm")
    time_rank = lax.axis_index("tm")
    owner_id = lax.axis_index("sta")
    factor_a = FACTOR_A
    factor_b = SAMPLES // FACTOR_A
    rows_local = factor_a // time_devices
    cols_local = factor_b // time_devices
    series = stations * hour_count
    arranged = records.reshape(series, rows_local, factor_b).transpose(1, 0, 2)
    spread = lax.all_to_all(arranged, "tm", split_axis=2, concat_axis=0, tiled=True)
    index_a = jnp.arange(factor_a, dtype=jnp.int32)
    index_b = jnp.arange(factor_b, dtype=jnp.int32)
    paired = rows_local == 2 * BAND and factor_a == 2 * BAND * time_devices
    if paired:
        owner_of_row = index_a // rows_local
        place_in_row = index_a % rows_local
        k1_order = jnp.where(
            place_in_row < BAND,
            BAND * owner_of_row + place_in_row,
            factor_a - BAND * (owner_of_row + 2) + place_in_row,
        )
        k1_ids = jnp.concatenate(
            [
                BAND * time_rank + jnp.arange(BAND, dtype=jnp.int32),
                factor_a - BAND * (time_rank + 1) + jnp.arange(BAND, dtype=jnp.int32),
            ]
        )
    else:
        k1_order = index_a
        k1_ids = time_rank * rows_local + jnp.arange(rows_local, dtype=jnp.int32)
    cosine_a, sine_a = angles(k1_order, index_a, factor_a)
    flat_rows = spread.reshape(factor_a, series * cols_local)
    both_a = jnp.concatenate([cosine_a, -sine_a], axis=0)
    section = matmul(both_a, flat_rows).reshape(2, factor_a, series, cols_local)
    section_real, section_imag = (section[0], section[1])
    col_global = time_rank * cols_local + jnp.arange(cols_local, dtype=jnp.int32)
    cosine_t, sine_t = angles(k1_order, col_global, SAMPLES)
    twisted_real = section_real * cosine_t[:, None, :] + section_imag * sine_t[:, None, :]
    twisted_imag = section_imag * cosine_t[:, None, :] - section_real * sine_t[:, None, :]
    twisted = jnp.stack([twisted_real, twisted_imag], axis=2)
    moved = lax.all_to_all(twisted, "tm", split_axis=0, concat_axis=3, tiled=True)
    cosine_b, sine_b = angles(index_b, index_b, factor_b)
    forward_b = jnp.concatenate(
        [jnp.concatenate([cosine_b, -sine_b], axis=1), jnp.concatenate([sine_b, cosine_b], axis=1)],
        axis=0,
    )
    spec = matmul(moved.reshape(rows_local * series, 2 * factor_b), forward_b)
    banded = spec.reshape(rows_local // BAND, BAND, series, 2, factor_b)
    band_power = jnp.mean(
        banded[:, :, :, 0] * banded[:, :, :, 0] + banded[:, :, :, 1] * banded[:, :, :, 1],
        axis=1,
        keepdims=True,
    )
    band_scale = lax.rsqrt(band_power + epsilon)
    whitened = (banded * band_scale[:, :, :, None]).reshape(rows_local, series, 2, factor_b)
    if paired:
        scale_row = band_scale[:, 0].transpose(1, 0, 2)[None]
        sent = jnp.concatenate(
            [spec.reshape(rows_local, series, 2, factor_b)[: BAND + 1], scale_row]
        )

        def rebuilt(piece):
            spec_part = piece[: BAND + 1]
            scale_low = piece[BAND + 1, :, 0][None, :, None, :]
            scale_high = piece[BAND + 1, :, 1][None, :, None, :]
            conj_sign = (1 - 2 * lax.iota(jnp.int32, 2)).astype(jnp.float32)[None, None, :, None]
            mirrored = spec_part[1:BAND][::-1, :, :, ::-1] * conj_sign
            high = jnp.concatenate([spec_part[BAND:], mirrored])
            return jnp.concatenate([spec_part[:BAND] * scale_low, high * scale_high])

    else:
        sent = whitened

        def rebuilt(piece):
            return piece

    pieces = [whitened]
    for distance in range(1, REACH + 1):
        pieces.append(rebuilt(passed_along(sent, "sta", -distance)))
    nearby = jnp.stack(pieces).reshape(REACH + 1, rows_local, stations, hour_count, 2, factor_b)
    slot_total = pair_blocks.shape[0]
    first_off = pair_blocks[:, 0] - owner_id
    second_off = pair_blocks[:, 1] - owner_id
    left_spec = jnp.stack(
        [
            lax.dynamic_index_in_dim(nearby, first_off[s], 0, keepdims=False)
            for s in range(slot_total)
        ]
    )
    right_spec = jnp.stack(
        [
            lax.dynamic_index_in_dim(nearby, second_off[s], 0, keepdims=False)
            for s in range(slot_total)
        ]
    )
    left_real = left_spec[:, :, :, None, :, 0]
    left_imag = left_spec[:, :, :, None, :, 1]
    right_real = right_spec[:, :, None, :, :, 0]
    right_imag = right_spec[:, :, None, :, :, 1]
    cross_real = jnp.sum(left_real * right_real + left_imag * right_imag, axis=4)
    cross_imag = jnp.sum(left_imag * right_real - left_real * right_imag, axis=4)
    cross = jnp.concatenate([cross_real, cross_imag], axis=-1)
    inverse_b = jnp.concatenate(
        [jnp.concatenate([cosine_b, sine_b], axis=1), jnp.concatenate([-sine_b, cosine_b], axis=1)],
        axis=0,
    )
    lag = matmul(cross.reshape(-1, 2 * factor_b), inverse_b).reshape(
        slot_total, rows_local, stations, stations, 2, factor_b
    )
    lag_real, lag_imag = (lag[:, :, :, :, 0], lag[:, :, :, :, 1])
    cosine_u, sine_u = angles(k1_ids, index_b, SAMPLES)
    turn_real = (
        lag_real * cosine_u[None, :, None, None, :] - lag_imag * sine_u[None, :, None, None, :]
    )
    turn_imag = (
        lag_real * sine_u[None, :, None, None, :] + lag_imag * cosine_u[None, :, None, None, :]
    )
    lag_ids = jnp.concatenate(
        [jnp.arange(LAGS, dtype=jnp.int32), factor_a - LAGS + jnp.arange(LAGS, dtype=jnp.int32)]
    )
    cosine_l, sine_l = angles(lag_ids, k1_ids, factor_a)
    lag_weights = jnp.concatenate([cosine_l, -sine_l], axis=1).reshape(
        time_devices, 2 * LAGS // time_devices, 2 * rows_local
    )
    turned = jnp.concatenate([turn_real, turn_imag], axis=1)
    scale_out = 1.0 / math.sqrt(SAMPLES * hour_count)
    live_mask = (jnp.arange(slot_total) < pair_count[0]).astype(jnp.float32) * scale_out
    lag_block = jnp.einsum(
        "dwp,spijm->dsijwm",
        lag_weights,
        turned,
        precision=highest,
        preferred_element_type=jnp.float32,
    )
    lag_block = lag_block * live_mask[None, :, None, None, None, None]
    gathered = lax.all_to_all(lag_block, "tm", split_axis=0, concat_axis=0, tiled=True)
    total = jnp.sum(gathered, axis=0)
    return total.reshape(slot_total, stations, stations, 2 * LAGS * factor_b // time_devices)


def solution(mesh):
    placed = (P("sta", None, "tm"), P("sta", None), P("sta"))
    return jax.shard_map(
        local, mesh=mesh, in_specs=placed, out_specs=P("sta", None, None, "tm"), check_vma=False
    )
```

profile of v0, /device:TPU:2, one launch (start us, length us, event | category | flops | bytes accessed | tf_op | source)
XLA Modules:
  0.0 73.7 jit_solution(5561566885266259954)
XLA Ops:
  0.0 1.3 %reduce.1 = f32[2,16384]{1,0:T(2,128)S(1)} reduce(f32[2,1,16384]{2,1,0:T(1,128)} %param.3, f32[]{:T(128)} %constant.136), dimensions={1}, to_apply=%param.3.reduce_sub_computation | reduce | bytes 262148 | tf_op args[0]
  1.5 0.9 %reshape.339 = f32[4,1,8192]{2,1,0:T(1,128)} reshape(f32[256,2,64]{2,1,0:T(2,128)S(1)} %bitcast.123) | data formatting | bytes 262144
  2.4 3.3 %all-to-all-start = ((f32[4,1,8192]{2,1,0:T(1,128)}), f32[4,1,8192]{2,1,0:T(1,128)S(1)}, u32[]{:S(2)}, u32[]{:S(2)}) async-start(f32[4,1,8192]{2,1,0:T(1,128)} %reshape.339), calls=%async_computation | async-start | bytes 262144 | tf_op jit(solution)/shard_map/all_to_all | solution.py:43
  5.7 1.0 %fusion.31 = (f32[256,256]{0,1:T(8,128)S(1)}, f32[256,256]{0,1:T(8,128)S(1)}) fusion(), kind=kLoop, calls=%fused_computation.80 | loop fusion | flops 917504 | bytes 524288 | tf_op jit(solution)/shard_map/sin | solution.py:25
  6.8 1.0 %fusion.35 = f32[256,256]{0,1:T(8,128)S(1)} fusion(), kind=kLoop, calls=%fused_computation.87 | loop fusion | flops 983040 | bytes 262144 | tf_op jit(solution)/shard_map/neg | solution.py:77
  7.8 0.7 fusion.66
  16.1 1.0 %fusion.33 = (f32[256,256]{0,1:T(8,128)S(1)}, f32[256,256]{0,1:T(8,128)S(1)}) fusion(s32[256]{0:T(256)S(1)} %compare_select_fusion.1), kind=kLoop, calls=%fused_computation.82 | loop fusion | flops 983040 | bytes 525312 | tf_op jit(solution)/shard_map/cos | solution.py:25
  22.5 0.5 broadcast.457
  23.1 1.0 %reduce.2 = f32[4,8192]{1,0:T(4,128)S(1)} reduce(f32[4,1,8192]{2,1,0:T(1,128)S(1)} %all-to-all-done, f32[]{:T(128)} %broadcast.457), dimensions={1}, to_apply=%all_to_all.25.reduce_sub_computation | reduce | bytes 262148 | tf_op jit(solution)/shard_map/all_to_all | solution.py:43
  25.7 1.3 %reshape.341 = f32[4,1,16384]{2,1,0:T(1,128)} reshape(f32[256,2,2,64]{3,2,1,0:T(2,128)S(1)} %copy.50) | data formatting | bytes 524288
  27.0 3.4 %all-to-all-start.1 = ((f32[4,1,16384]{2,1,0:T(1,128)}), f32[4,1,16384]{2,1,0:T(1,128)S(1)}, u32[]{:S(2)}, u32[]{:S(2)}) async-start(f32[4,1,16384]{2,1,0:T(1,128)} %reshape.341), calls=%async_computation.1 | async-start | bytes 524288 | tf_op jit(solution)/shard_map/all_to_all | solution.py:74
  30.5 5.8 %all-to-all-done.1 = f32[4,1,16384]{2,1,0:T(1,128)S(1)} async-done(((f32[4,1,16384]{2,1,0:T(1,128)}), f32[4,1,16384]{2,1,0:T(1,128)S(1)}, u32[]{:S(2)}, u32[]{:S(2)}) %all-to-all-start.1) | async-done | bytes 262176 | tf_op jit(solution)/shard_map/all_to_all | solution.py:74
  36.4 1.4 %reduce.3 = f32[4,16384]{1,0:T(4,128)S(1)} reduce(f32[4,1,16384]{2,1,0:T(1,128)S(1)} %all-to-all-done.1, f32[]{:T(128)} %broadcast.457), dimensions={1}, to_apply=%all_to_all.28.reduce_sub_computation | reduce | bytes 524292 | tf_op jit(solution)/shard_map/all_to_all | solution.py:74
  38.8 1.2 %fusion.9 = f32[128,512]{1,0:T(8,128)S(1)} fusion(f32[128,512]{1,0:T(8,128)S(1)} %reshape.330, f32[256,256]{0,1:T(8,128)S(1)} %get-tuple-element.54, f32[256,256]{0,1:T(8,128)S(1)} %get-tuple-element.53, f32[256,256]{0,1:T(8,128)S(1)} %fusion.35), kind=kOutput, calls=%fused_computation.15 | convolution fusion | flops 403439616 | bytes 1310720 | tf_op jit(solution)/shard_map/dot_general | solution.py:29
  40.7 1.9 %collective-permute-start = (f32[34,2,2,256]{3,0,2,1:T(8,128)S(1)}, f32[34,2,2,256]{3,0,2,1:T(8,128)S(1)}, u32[]{:S(2)}, u32[]{:S(2)}) collective-permute-start(f32[34,2,2,256]{3,0,2,1:T(8,128)S(1)} %pad_maximum_fusion.9), channel_id=1, source_target_pairs={{4,0},{8,4},{12,8},{16,12},{20,16},{24,20},{28,24},{5,1},{9,5},{13... | collective-permute-start | bytes 417800 | tf_op jit(solution)/shard_map/ppermute | solution.py:19
  42.6 1.3 %collective-permute-start.1 = (f32[34,2,2,256]{3,0,2,1:T(8,128)S(1)}, f32[34,2,2,256]{3,0,2,1:T(8,128)S(1)}, u32[]{:S(2)}, u32[]{:S(2)}) collective-permute-start(f32[34,2,2,256]{3,0,2,1:T(8,128)S(1)} %pad_maximum_fusion.9), channel_id=1, source_target_pairs={{8,0},{12,4},{16,8},{20,12},{24,16},{28,20},{9,1},{13,5},{17,9},{2... | collective-permute-start | bytes 417800 | tf_op jit(solution)/shard_map/ppermute | solution.py:19
  43.9 1.5 %collective-permute-start.2 = (f32[34,2,2,256]{3,0,2,1:T(8,128)S(1)}, f32[34,2,2,256]{3,0,2,1:T(8,128)S(1)}, u32[]{:S(2)}, u32[]{:S(2)}) collective-permute-start(f32[34,2,2,256]{3,0,2,1:T(8,128)S(1)} %pad_maximum_fusion.9), channel_id=1, source_target_pairs={{12,0},{16,4},{20,8},{24,12},{28,16},{13,1},{17,5},{21,9},{25,13},... | collective-permute-start | bytes 417800 | tf_op jit(solution)/shard_map/ppermute | solution.py:19
  45.6 4.9 %collective-permute-done = f32[34,2,2,256]{3,0,2,1:T(8,128)S(1)} collective-permute-done((f32[34,2,2,256]{3,0,2,1:T(8,128)S(1)}, f32[34,2,2,256]{3,0,2,1:T(8,128)S(1)}, u32[]{:S(2)}, u32[]{:S(2)}) %collective-permute-start) | collective-permute-done | bytes 139296 | tf_op jit(solution)/shard_map/ppermute | solution.py:19
  50.5 1.1 %collective-permute-done.1 = f32[34,2,2,256]{3,0,2,1:T(8,128)S(1)} collective-permute-done((f32[34,2,2,256]{3,0,2,1:T(8,128)S(1)}, f32[34,2,2,256]{3,0,2,1:T(8,128)S(1)}, u32[]{:S(2)}, u32[]{:S(2)}) %collective-permute-start.1) | collective-permute-done | bytes 139296 | tf_op jit(solution)/shard_map/ppermute | solution.py:19
  51.9 8.7 %collective-permute-done.2 = f32[34,2,2,256]{3,0,2,1:T(8,128)S(1)} collective-permute-done((f32[34,2,2,256]{3,0,2,1:T(8,128)S(1)}, f32[34,2,2,256]{3,0,2,1:T(8,128)S(1)}, u32[]{:S(2)}, u32[]{:S(2)}) %collective-permute-start.2) | collective-permute-done | bytes 139296 | tf_op jit(solution)/shard_map/ppermute | solution.py:19
  62.5 2.7 %fusion = f32[3,64,2,2,2,256]{5,1,4,3,2,0:T(8,128)S(1)} fusion(f32[2,256,512,1,1,1]{2,1,0,5,4,3:T(8,128)S(1)} %bitcast.120, f32[3,64,2,2,256]{4,1,3,2,0:T(8,128)S(1)} %get-tuple-element.8, f32[3,64,2,2,256]{4,1,3,2,0:T(8,128)S(1)} %get-tuple-element.7), kind=kOutput, calls=%fused_computation.1 | convolution fusion | flops 2416312320 | bytes 4194304 | tf_op jit(solution)/shard_map/dot_general | solution.py:29
  65.4 0.9 %fusion.7 = f32[4,3,2,2,2,256]{5,0,4,3,2,1:T(4,128)S(1)} fusion(f32[3,64,2,2,256]{4,1,3,2,0:T(8,128)S(1)} %get-tuple-element.6, f32[3,64,2,2,256]{4,1,3,2,0:T(8,128)S(1)} %get-tuple-element.5, f32[3]{0:T(128)S(1)} %compare_select_fusion, f32[4,2,64]{2,0,1:T(4,128)S(1)} %get-tuple-element.32, f32[4,2,64]{2,0,1:T(4,128)S(1)} %get-tuple-element.31), kind=kOutput, calls=%fused_computation.13 | convolution fusion | flops 38167552 | bytes 1675276 | tf_op jit(solution)/shard_map/dwp,spijm->dsijwm/dot_general | solution.py:161
  66.4 6.7 %all_to_all.35 = f32[4,3,2,2,2,256]{5,4,3,2,1,0:T(2,128)S(1)} all-to-all(f32[4,3,2,2,2,256]{5,4,3,2,1,0:T(2,128)S(1)} %copy.58), channel_id=1, replica_groups=mesh['sta'=8,'tm'=4] {'tm'}, dimensions={0} | all-to-all | bytes 196608 | tf_op jit(solution)/shard_map/all_to_all | solution.py:169
  73.1 0.6 reshape.333
  (80 shorter events, 7.0 us)
Async XLA Ops:
  0.0 7.8 %copy-start = (s32[3,2]{0,1:T(2,128)S(1)}, s32[3,2]{0,1:T(2,128)}, u32[]{:S(2)}) copy-start(s32[3,2]{0,1:T(2,128)} %param.4) | copy-start | bytes 76
  2.4 20.2 %all-to-all-start = ((f32[4,1,8192]{2,1,0:T(1,128)}), f32[4,1,8192]{2,1,0:T(1,128)S(1)}, u32[]{:S(2)}, u32[]{:S(2)}) async-start(f32[4,1,8192]{2,1,0:T(1,128)} %reshape.339), calls=%async_computation | async-start | bytes 262144 | tf_op jit(solution)/shard_map/all_to_all | solution.py:43
  27.0 9.4 %all-to-all-start.1 = ((f32[4,1,16384]{2,1,0:T(1,128)}), f32[4,1,16384]{2,1,0:T(1,128)S(1)}, u32[]{:S(2)}, u32[]{:S(2)}) async-start(f32[4,1,16384]{2,1,0:T(1,128)} %reshape.341), calls=%async_computation.1 | async-start | bytes 524288 | tf_op jit(solution)/shard_map/all_to_all | solution.py:74
  40.7 9.9 %collective-permute-start = (f32[34,2,2,256]{3,0,2,1:T(8,128)S(1)}, f32[34,2,2,256]{3,0,2,1:T(8,128)S(1)}, u32[]{:S(2)}, u32[]{:S(2)}) collective-permute-start(f32[34,2,2,256]{3,0,2,1:T(8,128)S(1)} %pad_maximum_fusion.9), channel_id=1, source_target_pairs={{4,0},{8,4},{12,8},{16,12},{20,16},{24,20},{28,24},{5,1},{9,5},{13... | collective-permute-start | bytes 417800 | tf_op jit(solution)/shard_map/ppermute | solution.py:19
  42.6 9.0 %collective-permute-start.1 = (f32[34,2,2,256]{3,0,2,1:T(8,128)S(1)}, f32[34,2,2,256]{3,0,2,1:T(8,128)S(1)}, u32[]{:S(2)}, u32[]{:S(2)}) collective-permute-start(f32[34,2,2,256]{3,0,2,1:T(8,128)S(1)} %pad_maximum_fusion.9), channel_id=1, source_target_pairs={{8,0},{12,4},{16,8},{20,12},{24,16},{28,20},{9,1},{13,5},{17,9},{2... | collective-permute-start | bytes 417800 | tf_op jit(solution)/shard_map/ppermute | solution.py:19
  43.9 16.7 %collective-permute-start.2 = (f32[34,2,2,256]{3,0,2,1:T(8,128)S(1)}, f32[34,2,2,256]{3,0,2,1:T(8,128)S(1)}, u32[]{:S(2)}, u32[]{:S(2)}) collective-permute-start(f32[34,2,2,256]{3,0,2,1:T(8,128)S(1)} %pad_maximum_fusion.9), channel_id=1, source_target_pairs={{12,0},{16,4},{20,8},{24,12},{28,16},{13,1},{17,5},{21,9},{25,13},... | collective-permute-start | bytes 417800 | tf_op jit(solution)/shard_map/ppermute | solution.py:19
where the time goes:
time: 74.3 us; the launch traced here: 73.7 us
  waiting for transfers between devices  20.5 us (28%)
  between operations  12.6 us (17%)
  starting transfers between devices  11.4 us (15%)
  other arithmetic  9.12 us (12%)
  local copies, waits for them, and re-layouts  8.13 us (11%)
  blocking collectives  6.67 us (9%)
  matrix products  5.25 us (7%)
    ppermute x3, waiting for transfers between devices, passed_along(): return lax.ppermute(block, axis, route)  14.7 us
    all_to_all x1, blocking collectives, local(): lax.all_to_all(lag_block, 'tm', split_axis=0, concat_axis=0, tiled=True)  6.67 us
    all_to_all x1, waiting for transfers between devices, local(): lax.all_to_all(twisted, 'tm', split_axis=0, concat_axis=3, tiled=True)  5.84 us
    ppermute x3, starting transfers between devices, passed_along(): return lax.ppermute(block, axis, route)  4.69 us
    dot_general x3, matrix products, matmul(): jnp.dot(left_mat, right_mat, precision=highest, preferred_element_type=jn...  4.32 us
    all_to_all x1, starting transfers between devices, local(): lax.all_to_all(twisted, 'tm', split_axis=0, concat_axis=3, tiled=True)  3.4 us
    all_to_all x1, starting transfers between devices, local(): lax.all_to_all(arranged, 'tm', split_axis=2, concat_axis=0, tiled=True)  3.32 us
    unnamed x13, local copies, waits for them, and re-layouts  2.85 us
  transfers between devices with their start and end apart: 5, of which 4 were waited for; matrix products, arithmetic and copies ran while one was open for 7% of the time, Pallas kernels for 0%

commit v1 on v0

--- a/solution.py
+++ b/solution.py
@@ -1,3 +1,4 @@
+import functools
 import math
 import jax
 import jax.numpy as jnp
@@ -11,6 +12,43 @@
 REACH = 3
 highest = lax.Precision.HIGHEST
 epsilon = 1e-06
+
+
+def _create_notes(buf, where_dim, obj):
+    n_now, z_new = (buf.shape[:where_dim], buf.shape[where_dim + 1 :])
+    r_now = buf.reshape(*n_now, obj, -1, *z_new)
+    current_arr = jnp.moveaxis(r_now, where_dim, 0)
+    return current_arr
+
+
+def note_the_inputs(sample, axis_no):
+    sample = jnp.moveaxis(sample, 0, axis_no)
+    aux = sample.shape
+    opened = sample.reshape(*aux[:axis_no], aux[axis_no] * aux[axis_no + 1], *aux[axis_no + 2 :])
+    return opened
+
+
+def review_numbers(packet, lane_axis, local_block, body):
+    out_arr = lax.axis_size(lane_axis)
+    x_new = lax.axis_index(lane_axis)
+    plain, t1 = (out_arr, x_new)
+    latest = _create_notes(packet, local_block, plain)
+    parts_seen = [latest[t1]]
+    hop_no = 1
+    while hop_no < plain:
+        part_now = latest[t1 ^ hop_no]
+        big = lax.ppermute(
+            part_now, axis_name=lane_axis, perm=[(u, u ^ hop_no) for u in range(plain)]
+        )
+        parts_seen.append(big)
+        hop_no = hop_no + 1
+    prior = jnp.stack(parts_seen, 0)
+    latest = prior[t1 ^ jnp.arange(plain)]
+    all_values = note_the_inputs(latest, body)
+    return all_values
+
+
+part_modes = functools.partial(review_numbers, lane_axis="tm", local_block=2, body=0)
 
 
 def passed_along(block, axis, distance):
@@ -40,7 +78,7 @@
     cols_local = factor_b // time_devices
     series = stations * hour_count
     arranged = records.reshape(series, rows_local, factor_b).transpose(1, 0, 2)
-    spread = lax.all_to_all(arranged, "tm", split_axis=2, concat_axis=0, tiled=True)
+    spread = part_modes(arranged)
     index_a = jnp.arange(factor_a, dtype=jnp.int32)
     index_b = jnp.arange(factor_b, dtype=jnp.int32)
     paired = rows_local == 2 * BAND and factor_a == 2 * BAND * time_devices

time: 74.3 us -> 71.5 us (0.962)
  starting transfers between devices: 11.4 us -> 10.3 us
  other arithmetic: 9.12 us -> 8.17 us
    all_to_all x1 -> x0, starting transfers between devices: 3.32 us -> none  [local(): lax.all_to_all(arranged, 'tm', split_axis=2, concat_axis=0, tiled=True)]
    ppermute x0 -> x3, starting transfers between devices: none -> 1.92 us  [review_numbers(): lax.ppermute(part_now, axis_name=lane_axis, perm=[(u, u ^ hop_no) for u i...]
    unnamed x13 -> x11, local copies, waits for them, and re-layouts: 2.85 us -> 1.71 us
    all_to_all x1 -> x0, other arithmetic: 0.98 us -> none  [local(): lax.all_to_all(arranged, 'tm', split_axis=2, concat_axis=0, tiled=True)]
    all_to_all x3 -> x0, local copies, waits for them, and re-layouts: 0.88 us -> none  [local(): lax.all_to_all(arranged, 'tm', split_axis=2, concat_axis=0, tiled=True)]
    gather x0 -> x2, local copies, waits for them, and re-layouts: none -> 0.77 us  [review_numbers(): latest = prior[t1 ^ jnp.arange(plain)]]
  transfers between devices with their start and end apart: 5 -> 7, of which waited for: 4 -> 4; matrix products, arithmetic and copies ran while one was open for 7% -> 7% of each run, Pallas kernels for 0% -> 0%
where the time goes in v1:
time: 71.5 us; the launch traced here: 71.1 us
  waiting for transfers between devices  20.4 us (29%)
  between operations  12.6 us (18%)
  starting transfers between devices  10.3 us (14%)
  other arithmetic  8.17 us (11%)
  local copies, waits for them, and re-layouts  7.61 us (11%)
  blocking collectives  6.67 us (9%)
  matrix products  5.25 us (7%)
    ppermute x3, waiting for transfers between devices, passed_along(): return lax.ppermute(block, axis, route)  14.6 us
    all_to_all x1, blocking collectives, local(): lax.all_to_all(lag_block, 'tm', split_axis=0, concat_axis=0, tiled=True)  6.67 us
    all_to_all x1, waiting for transfers between devices, local(): lax.all_to_all(twisted, 'tm', split_axis=0, concat_axis=3, tiled=True)  5.84 us
    ppermute x3, starting transfers between devices, passed_along(): return lax.ppermute(block, axis, route)  4.98 us
    dot_general x3, matrix products, matmul(): jnp.dot(left_mat, right_mat, precision=highest, preferred_element_type=jn...  4.32 us
    all_to_all x1, starting transfers between devices, local(): lax.all_to_all(twisted, 'tm', split_axis=0, concat_axis=3, tiled=True)  3.4 us
    ppermute x3, starting transfers between devices, review_numbers(): lax.ppermute(part_now, axis_name=lane_axis, perm=[(u, u ^ hop_no) for u i...  1.92 us
    cos x4, other arithmetic, angles(): return (jnp.cos(radians), jnp.sin(radians))  1.85 us
  transfers between devices with their start and end apart: 7, of which 4 were waited for; matrix products, arithmetic and copies ran while one was open for 7% of the time, Pallas kernels for 0%

profile of v1, /device:TPU:2, one launch (start us, length us, event | category | flops | bytes accessed | tf_op | source)
XLA Modules:
  0.0 71.1 jit_solution(10604396756739040704)
XLA Ops:
  0.0 1.3 %reduce.1 = f32[2,16384]{1,0:T(2,128)S(1)} reduce(f32[2,1,16384]{2,1,0:T(1,128)} %param.3, f32[]{:T(128)} %constant.143), dimensions={1}, to_apply=%param.3.reduce_sub_computation | reduce | bytes 262148 | tf_op args[0]
  1.8 1.6 %collective-permute-start.1 = (f32[64,2,64]{2,0,1:T(8,128)S(1)}, f32[64,2,64]{2,0,1:T(8,128)S(1)}, u32[]{:S(2)}, u32[]{:S(2)}) collective-permute-start(f32[64,2,64]{2,0,1:T(8,128)S(1)} %bitcast.137), channel_id=1, source_target_pairs={{0,2},{1,3},{2,0},{3,1},{4,6},{5,7},{6,4},{7,5},{8,10},{9,11},{10,... | collective-permute-start | bytes 98312 | tf_op jit(solution)/shard_map/ppermute | solution.py:40
  3.7 1.0 %fusion.31 = (f32[256,256]{0,1:T(8,128)S(1)}, f32[256,256]{0,1:T(8,128)S(1)}) fusion(), kind=kLoop, calls=%fused_computation.82 | loop fusion | flops 917504 | bytes 524288 | tf_op jit(solution)/shard_map/sin | solution.py:63
  4.7 1.0 %fusion.35 = f32[256,256]{0,1:T(8,128)S(1)} fusion(), kind=kLoop, calls=%fused_computation.89 | loop fusion | flops 983040 | bytes 262144 | tf_op jit(solution)/shard_map/neg | solution.py:115
  5.7 1.0 %fusion.33 = (f32[256,256]{0,1:T(8,128)S(1)}, f32[256,256]{0,1:T(8,128)S(1)}) fusion(s32[256]{0:T(256)S(1)} %compare_select_fusion.2), kind=kLoop, calls=%fused_computation.84 | loop fusion | flops 983040 | bytes 525312 | tf_op jit(solution)/shard_map/cos | solution.py:63
  8.3 0.7 fusion.67
  20.5 0.6 gather_fusion
  21.5 0.5 fusion.14
  22.4 1.2 %reshape.369 = f32[4,1,16384]{2,1,0:T(1,128)} reshape(f32[256,2,2,64]{3,2,1,0:T(2,128)S(1)} %copy.41) | data formatting | bytes 524288
  23.6 3.4 %all-to-all-start = ((f32[4,1,16384]{2,1,0:T(1,128)}), f32[4,1,16384]{2,1,0:T(1,128)S(1)}, u32[]{:S(2)}, u32[]{:S(2)}) async-start(f32[4,1,16384]{2,1,0:T(1,128)} %reshape.369), calls=%async_computation | async-start | bytes 524288 | tf_op jit(solution)/shard_map/all_to_all | solution.py:112
  27.2 5.8 %all-to-all-done = f32[4,1,16384]{2,1,0:T(1,128)S(1)} async-done(((f32[4,1,16384]{2,1,0:T(1,128)}), f32[4,1,16384]{2,1,0:T(1,128)S(1)}, u32[]{:S(2)}, u32[]{:S(2)}) %all-to-all-start) | async-done | bytes 262176 | tf_op jit(solution)/shard_map/all_to_all | solution.py:112
  33.0 0.5 broadcast.492
  33.5 1.4 %reduce.2 = f32[4,16384]{1,0:T(4,128)S(1)} reduce(f32[4,1,16384]{2,1,0:T(1,128)S(1)} %all-to-all-done, f32[]{:T(128)} %broadcast.492), dimensions={1}, to_apply=%all_to_all.14.reduce_sub_computation | reduce | bytes 524292 | tf_op jit(solution)/shard_map/all_to_all | solution.py:112
  36.0 1.2 %fusion.9 = f32[128,512]{1,0:T(8,128)S(1)} fusion(f32[128,512]{1,0:T(8,128)S(1)} %reshape.352, f32[256,256]{0,1:T(8,128)S(1)} %get-tuple-element.58, f32[256,256]{0,1:T(8,128)S(1)} %get-tuple-element.57, f32[256,256]{0,1:T(8,128)S(1)} %fusion.35), kind=kOutput, calls=%fused_computation.16 | convolution fusion | flops 403439616 | bytes 1310720 | tf_op jit(solution)/shard_map/dot_general | solution.py:67
  38.0 2.2 %collective-permute-start.3 = (f32[34,2,2,256]{3,0,2,1:T(8,128)S(1)}, f32[34,2,2,256]{3,0,2,1:T(8,128)S(1)}, u32[]{:S(2)}, u32[]{:S(2)}) collective-permute-start(f32[34,2,2,256]{3,0,2,1:T(8,128)S(1)} %pad_maximum_fusion.10), channel_id=1, source_target_pairs={{4,0},{8,4},{12,8},{16,12},{20,16},{24,20},{28,24},{5,1},{9,5},{13... | collective-permute-start | bytes 417800 | tf_op jit(solution)/shard_map/ppermute | solution.py:57
  40.2 1.3 %collective-permute-start.4 = (f32[34,2,2,256]{3,0,2,1:T(8,128)S(1)}, f32[34,2,2,256]{3,0,2,1:T(8,128)S(1)}, u32[]{:S(2)}, u32[]{:S(2)}) collective-permute-start(f32[34,2,2,256]{3,0,2,1:T(8,128)S(1)} %pad_maximum_fusion.10), channel_id=1, source_target_pairs={{8,0},{12,4},{16,8},{20,12},{24,16},{28,20},{9,1},{13,5},{17,9},{2... | collective-permute-start | bytes 417800 | tf_op jit(solution)/shard_map/ppermute | solution.py:57
  41.5 1.5 %collective-permute-start.5 = (f32[34,2,2,256]{3,0,2,1:T(8,128)S(1)}, f32[34,2,2,256]{3,0,2,1:T(8,128)S(1)}, u32[]{:S(2)}, u32[]{:S(2)}) collective-permute-start(f32[34,2,2,256]{3,0,2,1:T(8,128)S(1)} %pad_maximum_fusion.10), channel_id=1, source_target_pairs={{12,0},{16,4},{20,8},{24,12},{28,16},{13,1},{17,5},{21,9},{25,13},... | collective-permute-start | bytes 417800 | tf_op jit(solution)/shard_map/ppermute | solution.py:57
  43.1 4.8 %collective-permute-done.3 = f32[34,2,2,256]{3,0,2,1:T(8,128)S(1)} collective-permute-done((f32[34,2,2,256]{3,0,2,1:T(8,128)S(1)}, f32[34,2,2,256]{3,0,2,1:T(8,128)S(1)}, u32[]{:S(2)}, u32[]{:S(2)}) %collective-permute-start.3) | collective-permute-done | bytes 139296 | tf_op jit(solution)/shard_map/ppermute | solution.py:57
  47.9 1.3 %collective-permute-done.4 = f32[34,2,2,256]{3,0,2,1:T(8,128)S(1)} collective-permute-done((f32[34,2,2,256]{3,0,2,1:T(8,128)S(1)}, f32[34,2,2,256]{3,0,2,1:T(8,128)S(1)}, u32[]{:S(2)}, u32[]{:S(2)}) %collective-permute-start.4) | collective-permute-done | bytes 139296 | tf_op jit(solution)/shard_map/ppermute | solution.py:57
  49.4 8.6 %collective-permute-done.5 = f32[34,2,2,256]{3,0,2,1:T(8,128)S(1)} collective-permute-done((f32[34,2,2,256]{3,0,2,1:T(8,128)S(1)}, f32[34,2,2,256]{3,0,2,1:T(8,128)S(1)}, u32[]{:S(2)}, u32[]{:S(2)}) %collective-permute-start.5) | collective-permute-done | bytes 139296 | tf_op jit(solution)/shard_map/ppermute | solution.py:57
  59.8 2.7 %fusion = f32[3,64,2,2,2,256]{5,1,4,3,2,0:T(8,128)S(1)} fusion(f32[2,256,512,1,1,1]{2,1,0,5,4,3:T(8,128)S(1)} %bitcast.127, f32[3,64,2,2,256]{4,1,3,2,0:T(8,128)S(1)} %get-tuple-element.8, f32[3,64,2,2,256]{4,1,3,2,0:T(8,128)S(1)} %get-tuple-element.7), kind=kOutput, calls=%fused_computation.2 | convolution fusion | flops 2416312320 | bytes 4194304 | tf_op jit(solution)/shard_map/dot_general | solution.py:67
  62.7 0.9 %fusion.7 = f32[4,3,2,2,2,256]{5,0,4,3,2,1:T(4,128)S(1)} fusion(f32[3,64,2,2,256]{4,1,3,2,0:T(8,128)S(1)} %get-tuple-element.6, f32[3,64,2,2,256]{4,1,3,2,0:T(8,128)S(1)} %get-tuple-element.5, f32[3]{0:T(128)S(1)} %compare_select_fusion.1, f32[4,2,64]{2,0,1:T(4,128)S(1)} %get-tuple-element.36, f32[4,2,64]{2,0,1:T(4,128)S(1)} %get-tuple-element.35), kind=kOutput, calls=%fused_computation.14 | convolution fusion | flops 38167552 | bytes 1675276 | tf_op jit(solution)/shard_map/dwp,spijm->dsijwm/dot_general | solution.py:199
  63.7 6.7 %all_to_all.20 = f32[4,3,2,2,2,256]{5,4,3,2,1,0:T(2,128)S(1)} all-to-all(f32[4,3,2,2,2,256]{5,4,3,2,1,0:T(2,128)S(1)} %copy.49), channel_id=1, replica_groups=mesh['sta'=8,'tm'=4] {'tm'}, dimensions={0} | all-to-all | bytes 196608 | tf_op jit(solution)/shard_map/all_to_all | solution.py:207
  70.4 0.6 reshape.355
  (85 shorter events, 6.8 us)
Async XLA Ops:
  0.0 8.2 %copy-start = (s32[3,2]{0,1:T(2,128)S(1)}, s32[3,2]{0,1:T(2,128)}, u32[]{:S(2)}) copy-start(s32[3,2]{0,1:T(2,128)} %param.4) | copy-start | bytes 76
  1.7 18.7 %collective-permute-start = (f32[64,2,64]{2,0,1:T(8,128)S(1)}, f32[64,2,64]{2,0,1:T(8,128)S(1)}, u32[]{:S(2)}, u32[]{:S(2)}) collective-permute-start(f32[64,2,64]{2,0,1:T(8,128)S(1)} %bitcast.139), channel_id=1, source_target_pairs={{0,1},{1,0},{2,3},{3,2},{4,5},{5,4},{6,7},{7,6},{8,9},{9,8},{10,11... | collective-permute-start | bytes 98312 | tf_op jit(solution)/shard_map/ppermute | solution.py:40
  1.8 18.6 %collective-permute-start.1 = (f32[64,2,64]{2,0,1:T(8,128)S(1)}, f32[64,2,64]{2,0,1:T(8,128)S(1)}, u32[]{:S(2)}, u32[]{:S(2)}) collective-permute-start(f32[64,2,64]{2,0,1:T(8,128)S(1)} %bitcast.137), channel_id=1, source_target_pairs={{0,2},{1,3},{2,0},{3,1},{4,6},{5,7},{6,4},{7,5},{8,10},{9,11},{10,... | collective-permute-start | bytes 98312 | tf_op jit(solution)/shard_map/ppermute | solution.py:40
  3.4 17.1 %collective-permute-start.2 = (f32[64,2,64]{2,0,1:T(8,128)S(1)}, f32[64,2,64]{2,0,1:T(8,128)S(1)}, u32[]{:S(2)}, u32[]{:S(2)}) collective-permute-start(f32[64,2,64]{2,0,1:T(8,128)S(1)} %bitcast.136), channel_id=1, source_target_pairs={{0,3},{1,2},{2,1},{3,0},{4,7},{5,6},{6,5},{7,4},{8,11},{9,10},{10,... | collective-permute-start | bytes 98312 | tf_op jit(solution)/shard_map/ppermute | solution.py:40
  23.6 9.4 %all-to-all-start = ((f32[4,1,16384]{2,1,0:T(1,128)}), f32[4,1,16384]{2,1,0:T(1,128)S(1)}, u32[]{:S(2)}, u32[]{:S(2)}) async-start(f32[4,1,16384]{2,1,0:T(1,128)} %reshape.369), calls=%async_computation | async-start | bytes 524288 | tf_op jit(solution)/shard_map/all_to_all | solution.py:112
  38.0 9.9 %collective-permute-start.3 = (f32[34,2,2,256]{3,0,2,1:T(8,128)S(1)}, f32[34,2,2,256]{3,0,2,1:T(8,128)S(1)}, u32[]{:S(2)}, u32[]{:S(2)}) collective-permute-start(f32[34,2,2,256]{3,0,2,1:T(8,128)S(1)} %pad_maximum_fusion.10), channel_id=1, source_target_pairs={{4,0},{8,4},{12,8},{16,12},{20,16},{24,20},{28,24},{5,1},{9,5},{13... | collective-permute-start | bytes 417800 | tf_op jit(solution)/shard_map/ppermute | solution.py:57
  40.2 8.9 %collective-permute-start.4 = (f32[34,2,2,256]{3,0,2,1:T(8,128)S(1)}, f32[34,2,2,256]{3,0,2,1:T(8,128)S(1)}, u32[]{:S(2)}, u32[]{:S(2)}) collective-permute-start(f32[34,2,2,256]{3,0,2,1:T(8,128)S(1)} %pad_maximum_fusion.10), channel_id=1, source_target_pairs={{8,0},{12,4},{16,8},{20,12},{24,16},{28,20},{9,1},{13,5},{17,9},{2... | collective-permute-start | bytes 417800 | tf_op jit(solution)/shard_map/ppermute | solution.py:57
  41.5 16.5 %collective-permute-start.5 = (f32[34,2,2,256]{3,0,2,1:T(8,128)S(1)}, f32[34,2,2,256]{3,0,2,1:T(8,128)S(1)}, u32[]{:S(2)}, u32[]{:S(2)}) collective-permute-start(f32[34,2,2,256]{3,0,2,1:T(8,128)S(1)} %pad_maximum_fusion.10), channel_id=1, source_target_pairs={{12,0},{16,4},{20,8},{24,12},{28,16},{13,1},{17,5},{21,9},{25,13},... | collective-permute-start | bytes 417800 | tf_op jit(solution)/shard_map/ppermute | solution.py:57
